TPU v7x, 512 devices: a whole 4x8x8 slice. The times are simulated.
512 devices in a mesh: ctxlo: 16 (over z_hi, x), ctxhi: 32 (over y, z_lo, core).
Axes of the slice: x: 4, y: 8, z: 8 (z_hi: 4, z_lo: 2; z = z_hi * 2 + z_lo), core: 2. Of those that a mesh axis runs over, the one named last changes fastest.
Arguments:
- key_value: bfloat16 [32, 16, 384, 256], P('ctxhi', 'ctxlo'), may hold values from -6 to 6
- queries: bfloat16 [32, 16, 384, 768], P('ctxhi', 'ctxlo'), may hold values from -300 to 300
Outputs:
- attended: bfloat16 [32, 16, 384, 768], P('ctxhi', 'ctxlo')
All inputs are finite; a program needn't handle non-finite values.
Results may differ from a plain program's by a relative error of at most 0.0038.
Values may be sent and summed in bfloat16 or wider, within the bound.
No kernel may reach another device: no remote copies, remote signals or barrier semaphores. Data moves between devices by JAX's collectives and lax.ppermute only.
A program may use at most 64 MiB of HBM per device.

v0:
```python
import math

import jax
import jax.numpy as jnp
from jax import lax
from jax.experimental import pallas as pl
from jax.sharding import PartitionSpec as P

HQ = 6
LAUNCH_ORDER = (
    ("ctxhi", 4), ("ctxhi", 3), ("ctxlo", 3), ("ctxlo", 2), ("ctxlo", 1),
    ("ctxhi", 2), ("ctxhi", 1), ("ctxlo", 0), ("ctxhi", 0),
)


def swapped(block, axis, stride):
    count = lax.axis_size(axis)
    route = []
    for low in range(count):
        high = low | 1 << stride
        if high != low and high < count:
            route += [(low, high), (high, low)]
    return lax.ppermute(block, axis, route)


def attend_kernel(*refs):
    q_ref = refs[0]
    kv_refs = refs[1:-1]
    o_ref = refs[-1]
    tokens = q_ref.shape[0]
    head_size = kv_refs[0].shape[1] // 2
    heads = q_ref.shape[1] // head_size
    scale = 1.0 / math.sqrt(head_size)
    query = jnp.concatenate(
        [q_ref[:, h * head_size:(h + 1) * head_size] for h in range(heads)], axis=0
    )
    scores = []
    top = None
    for kv_ref in kv_refs:
        block = lax.dot_general(
            kv_ref[:, :head_size], query, (((1,), (1,)), ((), ())),
            preferred_element_type=jnp.float32,
        )
        scores.append(block)
        block_top = jnp.max(block, axis=0, keepdims=True)
        top = block_top if top is None else jnp.maximum(top, block_top)
    summed = None
    total = None
    for kv_ref, block in zip(kv_refs, scores):
        expo = jnp.exp2((block - top) * (scale * math.log2(math.e)))
        block_total = jnp.sum(expo, axis=0, keepdims=True)
        total = block_total if total is None else total + block_total
        update = lax.dot_general(
            kv_ref[:, head_size:], expo.astype(jnp.bfloat16), (((0,), (0,)), ((), ())),
            preferred_element_type=jnp.float32,
        )
        summed = update if summed is None else summed + update
    result = (summed / total).T.astype(o_ref.dtype)
    for h in range(heads):
        o_ref[:, h * head_size:(h + 1) * head_size] = result[h * tokens:(h + 1) * tokens]


def attend(query, blocks):
    tokens, width = query.shape
    kv_spec = pl.BlockSpec(blocks[0].shape, lambda i: (0, 0))
    return pl.pallas_call(
        attend_kernel,
        out_shape=jax.ShapeDtypeStruct((tokens, width), jnp.bfloat16),
        grid=(1,),
        in_specs=[pl.BlockSpec((tokens, width), lambda i: (0, 0))] + [kv_spec] * len(blocks),
        out_specs=pl.BlockSpec((tokens, width), lambda i: (0, 0)),
    )(query, *blocks)


def per_device(key_value, queries):
    tokens = key_value.shape[2]
    pair = key_value.shape[3]
    local_kv = key_value.reshape(tokens, pair)
    query = queries.reshape(tokens, queries.shape[3])
    blocks = [local_kv]
    for axis, bit in LAUNCH_ORDER[::-1]:
        blocks.append(swapped(local_kv, axis, bit))
    result = attend(query, blocks)
    return result.reshape(1, 1, tokens, queries.shape[3])


def solution(mesh):
    return jax.shard_map(
        per_device,
        mesh=mesh,
        in_specs=(P("ctxhi", "ctxlo", None, None), P("ctxhi", "ctxlo", None, None)),
        out_specs=P("ctxhi", "ctxlo", None, None),
        check_vma=False,
    )
```

profile of v0, /device:TPU:1, one launch (start us, length us, event | category | flops | bytes accessed | tf_op | source)
XLA Modules:
  0.0 59.6 jit_solution(13030764595235704760)
XLA Ops:
  0.0 8.3 %collective-permute-start.8 = (bf16[384,256]{1,0:T(8,128)(2,1)}, bf16[384,256]{1,0:T(8,128)(2,1)S(1)}, u32[]{:S(2)}, u32[]{:S(2)}) collective-permute-start(bf16[384,256]{1,0:T(8,128)(2,1)} %bitcast.4), channel_id=1, source_target_pairs={{0,16},{16,0},{1,17},{17,1},{2,18},{18,2},{3,19},{19,3},{4,20},{20... | collective-permute-start | bytes 589832 | tf_op jit(solution)/shard_map/ppermute | solution.py:23
  8.3 2.4 %collective-permute-start.7 = (bf16[384,256]{1,0:T(8,128)(2,1)}, bf16[384,256]{1,0:T(8,128)(2,1)S(1)}, u32[]{:S(2)}, u32[]{:S(2)}) collective-permute-start(bf16[384,256]{1,0:T(8,128)(2,1)} %bitcast.5), channel_id=1, source_target_pairs={{0,8},{8,0},{1,9},{9,1},{2,10},{10,2},{3,11},{11,3},{4,12},{12,4},... | collective-permute-start | bytes 589832 | tf_op jit(solution)/shard_map/ppermute | solution.py:23
  10.7 10.6 %collective-permute-start.6 = (bf16[384,256]{1,0:T(8,128)(2,1)}, bf16[384,256]{1,0:T(8,128)(2,1)S(1)}, u32[]{:S(2)}, u32[]{:S(2)}) collective-permute-start(bf16[384,256]{1,0:T(8,128)(2,1)} %bitcast.6), channel_id=1, source_target_pairs={{0,256},{256,0},{32,288},{288,32},{64,320},{320,64},{96,352},{352,... | collective-permute-start | bytes 589832 | tf_op jit(solution)/shard_map/ppermute | solution.py:23
  21.3 4.0 %collective-permute-start.5 = (bf16[384,256]{1,0:T(8,128)(2,1)}, bf16[384,256]{1,0:T(8,128)(2,1)S(1)}, u32[]{:S(2)}, u32[]{:S(2)}) collective-permute-start(bf16[384,256]{1,0:T(8,128)(2,1)} %bitcast.7), channel_id=1, source_target_pairs={{0,128},{128,0},{32,160},{160,32},{64,192},{192,64},{96,224},{224,... | collective-permute-start | bytes 589832 | tf_op jit(solution)/shard_map/ppermute | solution.py:23
  25.4 4.7 %collective-permute-start.4 = (bf16[384,256]{1,0:T(8,128)(2,1)}, bf16[384,256]{1,0:T(8,128)(2,1)S(1)}, u32[]{:S(2)}, u32[]{:S(2)}) collective-permute-start(bf16[384,256]{1,0:T(8,128)(2,1)} %bitcast.8), channel_id=1, source_target_pairs={{0,64},{64,0},{32,96},{96,32},{128,192},{192,128},{160,224},{224,1... | collective-permute-start | bytes 589832 | tf_op jit(solution)/shard_map/ppermute | solution.py:23
  30.0 0.0 collective-permute-done.8.refs_10_
  30.0 0.0 copy-start
  30.0 2.3 %collective-permute-start.3 = (bf16[384,256]{1,0:T(8,128)(2,1)}, bf16[384,256]{1,0:T(8,128)(2,1)S(1)}, u32[]{:S(2)}, u32[]{:S(2)}) collective-permute-start(bf16[384,256]{1,0:T(8,128)(2,1)} %bitcast.9), channel_id=1, source_target_pairs={{0,4},{4,0},{1,5},{5,1},{2,6},{6,2},{3,7},{7,3},{8,12},{12,8},{9,1... | collective-permute-start | bytes 589832 | tf_op jit(solution)/shard_map/ppermute | solution.py:23
  32.4 0.0 collective-permute-done.7.refs_9_
  32.4 0.0 copy-start.1
  32.4 3.1 %collective-permute-start.2 = (bf16[384,256]{1,0:T(8,128)(2,1)}, bf16[384,256]{1,0:T(8,128)(2,1)S(1)}, u32[]{:S(2)}, u32[]{:S(2)}) collective-permute-start(bf16[384,256]{1,0:T(8,128)(2,1)} %bitcast.10), channel_id=1, source_target_pairs={{0,2},{2,0},{1,3},{3,1},{4,6},{6,4},{5,7},{7,5},{8,10},{10,8},{9,1... | collective-permute-start | bytes 589832 | tf_op jit(solution)/shard_map/ppermute | solution.py:23
  35.5 0.0 collective-permute-done.6.refs_8_
  35.5 0.0 copy-start.2
  35.5 2.2 %collective-permute-start.1 = (bf16[384,256]{1,0:T(8,128)(2,1)}, bf16[384,256]{1,0:T(8,128)(2,1)S(1)}, u32[]{:S(2)}, u32[]{:S(2)}) collective-permute-start(bf16[384,256]{1,0:T(8,128)(2,1)} %bitcast.11), channel_id=1, source_target_pairs={{0,32},{32,0},{64,96},{96,64},{128,160},{160,128},{192,224},{224,1... | collective-permute-start | bytes 589832 | tf_op jit(solution)/shard_map/ppermute | solution.py:23
  37.7 3.0 %collective-permute-done.5.refs_7_ = bf16[384,256]{1,0:T(8,128)(2,1)S(1)} collective-permute-done((bf16[384,256]{1,0:T(8,128)(2,1)}, bf16[384,256]{1,0:T(8,128)(2,1)S(1)}, u32[]{:S(2)}, u32[]{:S(2)}) %collective-permute-start.5) | collective-permute-done | bytes 196640 | tf_op jit(solution)/shard_map/ppermute | solution.py:23
  40.7 0.0 copy-start.3
  40.7 2.5 %collective-permute-start = (bf16[384,256]{1,0:T(8,128)(2,1)}, bf16[384,256]{1,0:T(8,128)(2,1)S(1)}, u32[]{:S(2)}, u32[]{:S(2)}) collective-permute-start(bf16[384,256]{1,0:T(8,128)(2,1)} %bitcast.12), channel_id=1, source_target_pairs={{0,1},{1,0},{2,3},{3,2},{4,5},{5,4},{6,7},{7,6},{8,9},{9,8},{10,11... | collective-permute-start | bytes 589832 | tf_op jit(solution)/shard_map/ppermute | solution.py:23
  43.2 0.0 collective-permute-done.4.refs_6_
  43.2 0.0 copy-start.4
  43.2 0.0 collective-permute-done.3.refs_5_
  43.2 0.0 copy-start.5
  43.2 1.7 %collective-permute-done.2.refs_4_ = bf16[384,256]{1,0:T(8,128)(2,1)S(1)} collective-permute-done((bf16[384,256]{1,0:T(8,128)(2,1)}, bf16[384,256]{1,0:T(8,128)(2,1)S(1)}, u32[]{:S(2)}, u32[]{:S(2)}) %collective-permute-start.2) | collective-permute-done | bytes 196640 | tf_op jit(solution)/shard_map/ppermute | solution.py:23
  44.9 0.0 copy-start.6
  44.9 0.0 collective-permute-done.1.refs_3_
  44.9 0.0 copy-start.7
  44.9 0.0 collective-permute-done.refs_2_
  44.9 0.0 copy-start.8
  44.9 0.0 copy-done
  44.9 0.0 copy-done.1
  44.9 0.0 copy-done.2
  44.9 0.0 copy-done.3
  44.9 0.0 copy-done.4
  45.0 0.0 copy-done.5
  45.0 0.6 copy-done.6
  45.6 0.1 copy-done.7
  45.6 0.1 copy-done.8
  45.7 13.9 %shard_map.28 = bf16[384,768]{1,0:T(8,128)(2,1)} custom-call(bf16[384,768]{1,0:T(8,128)(2,1)} %bitcast.3, bf16[384,256]{1,0:T(8,128)(2,1)} %bitcast.13, bf16[384,256]{1,0:T(8,128)(2,1)} %copy-done.8, bf16[384,256]{1,0:T(8,128)(2,1)} %copy-done.7, bf16[384,256]{1,0:T(8,128)(2,1)} %copy-done.6, bf16[384,256]{1,0:T(8,128)(2,1)} %copy-done.5, ...), custom_call_target="tpu_custom_call" | custom-call | tf_op jit(solution)/shard_map/pallas_call | solution.py:66
Async XLA Ops:
  0.0 30.0 %collective-permute-start.8 = (bf16[384,256]{1,0:T(8,128)(2,1)}, bf16[384,256]{1,0:T(8,128)(2,1)S(1)}, u32[]{:S(2)}, u32[]{:S(2)}) collective-permute-start(bf16[384,256]{1,0:T(8,128)(2,1)} %bitcast.4), channel_id=1, source_target_pairs={{0,16},{16,0},{1,17},{17,1},{2,18},{18,2},{3,19},{19,3},{4,20},{20... | collective-permute-start | bytes 589832 | tf_op jit(solution)/shard_map/ppermute | solution.py:23
  8.3 24.1 %collective-permute-start.7 = (bf16[384,256]{1,0:T(8,128)(2,1)}, bf16[384,256]{1,0:T(8,128)(2,1)S(1)}, u32[]{:S(2)}, u32[]{:S(2)}) collective-permute-start(bf16[384,256]{1,0:T(8,128)(2,1)} %bitcast.5), channel_id=1, source_target_pairs={{0,8},{8,0},{1,9},{9,1},{2,10},{10,2},{3,11},{11,3},{4,12},{12,4},... | collective-permute-start | bytes 589832 | tf_op jit(solution)/shard_map/ppermute | solution.py:23
  10.7 24.8 %collective-permute-start.6 = (bf16[384,256]{1,0:T(8,128)(2,1)}, bf16[384,256]{1,0:T(8,128)(2,1)S(1)}, u32[]{:S(2)}, u32[]{:S(2)}) collective-permute-start(bf16[384,256]{1,0:T(8,128)(2,1)} %bitcast.6), channel_id=1, source_target_pairs={{0,256},{256,0},{32,288},{288,32},{64,320},{320,64},{96,352},{352,... | collective-permute-start | bytes 589832 | tf_op jit(solution)/shard_map/ppermute | solution.py:23
  21.3 19.4 %collective-permute-start.5 = (bf16[384,256]{1,0:T(8,128)(2,1)}, bf16[384,256]{1,0:T(8,128)(2,1)S(1)}, u32[]{:S(2)}, u32[]{:S(2)}) collective-permute-start(bf16[384,256]{1,0:T(8,128)(2,1)} %bitcast.7), channel_id=1, source_target_pairs={{0,128},{128,0},{32,160},{160,32},{64,192},{192,64},{96,224},{224,... | collective-permute-start | bytes 589832 | tf_op jit(solution)/shard_map/ppermute | solution.py:23
  25.4 17.8 %collective-permute-start.4 = (bf16[384,256]{1,0:T(8,128)(2,1)}, bf16[384,256]{1,0:T(8,128)(2,1)S(1)}, u32[]{:S(2)}, u32[]{:S(2)}) collective-permute-start(bf16[384,256]{1,0:T(8,128)(2,1)} %bitcast.8), channel_id=1, source_target_pairs={{0,64},{64,0},{32,96},{96,32},{128,192},{192,128},{160,224},{224,1... | collective-permute-start | bytes 589832 | tf_op jit(solution)/shard_map/ppermute | solution.py:23
  30.0 14.9 %copy-start = (bf16[384,256]{1,0:T(8,128)(2,1)}, bf16[384,256]{1,0:T(8,128)(2,1)S(1)}, u32[]{:S(2)}) copy-start(bf16[384,256]{1,0:T(8,128)(2,1)S(1)} %collective-permute-done.8.refs_10_) | copy-start | bytes 589828
  30.0 13.2 %collective-permute-start.3 = (bf16[384,256]{1,0:T(8,128)(2,1)}, bf16[384,256]{1,0:T(8,128)(2,1)S(1)}, u32[]{:S(2)}, u32[]{:S(2)}) collective-permute-start(bf16[384,256]{1,0:T(8,128)(2,1)} %bitcast.9), channel_id=1, source_target_pairs={{0,4},{4,0},{1,5},{5,1},{2,6},{6,2},{3,7},{7,3},{8,12},{12,8},{9,1... | collective-permute-start | bytes 589832 | tf_op jit(solution)/shard_map/ppermute | solution.py:23
  32.4 12.6 %copy-start.1 = (bf16[384,256]{1,0:T(8,128)(2,1)}, bf16[384,256]{1,0:T(8,128)(2,1)S(1)}, u32[]{:S(2)}) copy-start(bf16[384,256]{1,0:T(8,128)(2,1)S(1)} %collective-permute-done.7.refs_9_) | copy-start | bytes 589828
  32.4 12.5 %collective-permute-start.2 = (bf16[384,256]{1,0:T(8,128)(2,1)}, bf16[384,256]{1,0:T(8,128)(2,1)S(1)}, u32[]{:S(2)}, u32[]{:S(2)}) collective-permute-start(bf16[384,256]{1,0:T(8,128)(2,1)} %bitcast.10), channel_id=1, source_target_pairs={{0,2},{2,0},{1,3},{3,1},{4,6},{6,4},{5,7},{7,5},{8,10},{10,8},{9,1... | collective-permute-start | bytes 589832 | tf_op jit(solution)/shard_map/ppermute | solution.py:23
  35.5 9.4 %copy-start.2 = (bf16[384,256]{1,0:T(8,128)(2,1)}, bf16[384,256]{1,0:T(8,128)(2,1)S(1)}, u32[]{:S(2)}) copy-start(bf16[384,256]{1,0:T(8,128)(2,1)S(1)} %collective-permute-done.6.refs_8_) | copy-start | bytes 589828
  35.5 9.4 %collective-permute-start.1 = (bf16[384,256]{1,0:T(8,128)(2,1)}, bf16[384,256]{1,0:T(8,128)(2,1)S(1)}, u32[]{:S(2)}, u32[]{:S(2)}) collective-permute-start(bf16[384,256]{1,0:T(8,128)(2,1)} %bitcast.11), channel_id=1, source_target_pairs={{0,32},{32,0},{64,96},{96,64},{128,160},{160,128},{192,224},{224,1... | collective-permute-start | bytes 589832 | tf_op jit(solution)/shard_map/ppermute | solution.py:23
  40.7 4.2 %copy-start.3 = (bf16[384,256]{1,0:T(8,128)(2,1)}, bf16[384,256]{1,0:T(8,128)(2,1)S(1)}, u32[]{:S(2)}) copy-start(bf16[384,256]{1,0:T(8,128)(2,1)S(1)} %collective-permute-done.5.refs_7_) | copy-start | bytes 589828
  40.7 4.2 %collective-permute-start = (bf16[384,256]{1,0:T(8,128)(2,1)}, bf16[384,256]{1,0:T(8,128)(2,1)S(1)}, u32[]{:S(2)}, u32[]{:S(2)}) collective-permute-start(bf16[384,256]{1,0:T(8,128)(2,1)} %bitcast.12), channel_id=1, source_target_pairs={{0,1},{1,0},{2,3},{3,2},{4,5},{5,4},{6,7},{7,6},{8,9},{9,8},{10,11... | collective-permute-start | bytes 589832 | tf_op jit(solution)/shard_map/ppermute | solution.py:23
  43.2 1.8 %copy-start.4 = (bf16[384,256]{1,0:T(8,128)(2,1)}, bf16[384,256]{1,0:T(8,128)(2,1)S(1)}, u32[]{:S(2)}) copy-start(bf16[384,256]{1,0:T(8,128)(2,1)S(1)} %collective-permute-done.4.refs_6_) | copy-start | bytes 589828
  43.2 1.8 %copy-start.5 = (bf16[384,256]{1,0:T(8,128)(2,1)}, bf16[384,256]{1,0:T(8,128)(2,1)S(1)}, u32[]{:S(2)}) copy-start(bf16[384,256]{1,0:T(8,128)(2,1)S(1)} %collective-permute-done.3.refs_5_) | copy-start | bytes 589828
  44.9 0.7 %copy-start.6 = (bf16[384,256]{1,0:T(8,128)(2,1)}, bf16[384,256]{1,0:T(8,128)(2,1)S(1)}, u32[]{:S(2)}) copy-start(bf16[384,256]{1,0:T(8,128)(2,1)S(1)} %collective-permute-done.2.refs_4_) | copy-start | bytes 589828
  44.9 0.8 %copy-start.7 = (bf16[384,256]{1,0:T(8,128)(2,1)}, bf16[384,256]{1,0:T(8,128)(2,1)S(1)}, u32[]{:S(2)}) copy-start(bf16[384,256]{1,0:T(8,128)(2,1)S(1)} %collective-permute-done.1.refs_3_) | copy-start | bytes 589828
  44.9 0.8 %copy-start.8 = (bf16[384,256]{1,0:T(8,128)(2,1)}, bf16[384,256]{1,0:T(8,128)(2,1)S(1)}, u32[]{:S(2)}) copy-start(bf16[384,256]{1,0:T(8,128)(2,1)S(1)} %collective-permute-done.refs_2_) | copy-start | bytes 589828
where the time goes:
time: 59.9 us; the launch traced here: 59.6 us
  starting transfers between devices  40.1 us (67%)
  Pallas kernels  13.9 us (23%)
  waiting for transfers between devices  4.66 us (8%)
  local copies, waits for them, and re-layouts  0.78 us (1%)
    ppermute x9, starting transfers between devices, swapped(): return lax.ppermute(block, axis, route)  40.1 us
    pallas_call x1, Pallas kernels, attend(): pl.pallas_call(attend_kernel, out_shape=jax.ShapeDtypeStruct((tokens, wid...  13.9 us
    ppermute x9, waiting for transfers between devices, swapped(): return lax.ppermute(block, axis, route)  4.66 us
  transfers between devices with their start and end apart: 9, of which 2 were waited for; matrix products, arithmetic and copies ran while one was open for 0% of the time, Pallas kernels for 0%

commit v1 on v0

--- a/solution.py
+++ b/solution.py
@@ -8,7 +8,7 @@
 
 HQ = 6
 LAUNCH_ORDER = (
-    ("ctxhi", 4), ("ctxhi", 3), ("ctxlo", 3), ("ctxlo", 2), ("ctxlo", 1),
+    ("ctxhi", 4), ("ctxlo", 3), ("ctxlo", 2), ("ctxhi", 3), ("ctxlo", 1),
     ("ctxhi", 2), ("ctxhi", 1), ("ctxlo", 0), ("ctxhi", 0),
 )
 

time: 59.9 us -> 61.2 us (1.022)
  starting transfers between devices: 40.1 us -> 41.3 us
    ppermute x9, starting transfers between devices: 40.1 us -> 41.3 us  [swapped(): return lax.ppermute(block, axis, route)]
where the time goes in v1:
time: 61.2 us; the launch traced here: 60.8 us
  starting transfers between devices  41.3 us (67%)
  Pallas kernels  13.8 us (23%)
  waiting for transfers between devices  4.73 us (8%)
  local copies, waits for them, and re-layouts  0.7 us (1%)
    ppermute x9, starting transfers between devices, swapped(): return lax.ppermute(block, axis, route)  41.3 us
    pallas_call x1, Pallas kernels, attend(): pl.pallas_call(attend_kernel, out_shape=jax.ShapeDtypeStruct((tokens, wid...  13.8 us
    ppermute x9, waiting for transfers between devices, swapped(): return lax.ppermute(block, axis, route)  4.73 us
  transfers between devices with their start and end apart: 9, of which 2 were waited for; matrix products, arithmetic and copies ran while one was open for 0% of the time, Pallas kernels for 0%

profile of v1, /device:TPU:1, one launch (start us, length us, event | category | flops | bytes accessed | tf_op | source)
XLA Modules:
  0.0 60.8 jit_solution(12236306235339683961)
XLA Ops:
  0.0 8.3 %collective-permute-start.8 = (bf16[384,256]{1,0:T(8,128)(2,1)}, bf16[384,256]{1,0:T(8,128)(2,1)S(1)}, u32[]{:S(2)}, u32[]{:S(2)}) collective-permute-start(bf16[384,256]{1,0:T(8,128)(2,1)} %bitcast.4), channel_id=1, source_target_pairs={{0,16},{16,0},{1,17},{17,1},{2,18},{18,2},{3,19},{19,3},{4,20},{20... | collective-permute-start | bytes 589832 | tf_op jit(solution)/shard_map/ppermute | solution.py:23
  8.3 10.6 %collective-permute-start.7 = (bf16[384,256]{1,0:T(8,128)(2,1)}, bf16[384,256]{1,0:T(8,128)(2,1)S(1)}, u32[]{:S(2)}, u32[]{:S(2)}) collective-permute-start(bf16[384,256]{1,0:T(8,128)(2,1)} %bitcast.5), channel_id=1, source_target_pairs={{0,256},{256,0},{32,288},{288,32},{64,320},{320,64},{96,352},{352,... | collective-permute-start | bytes 589832 | tf_op jit(solution)/shard_map/ppermute | solution.py:23
  18.9 4.0 %collective-permute-start.6 = (bf16[384,256]{1,0:T(8,128)(2,1)}, bf16[384,256]{1,0:T(8,128)(2,1)S(1)}, u32[]{:S(2)}, u32[]{:S(2)}) collective-permute-start(bf16[384,256]{1,0:T(8,128)(2,1)} %bitcast.6), channel_id=1, source_target_pairs={{0,128},{128,0},{32,160},{160,32},{64,192},{192,64},{96,224},{224,... | collective-permute-start | bytes 589832 | tf_op jit(solution)/shard_map/ppermute | solution.py:23
  22.9 2.4 %collective-permute-start.5 = (bf16[384,256]{1,0:T(8,128)(2,1)}, bf16[384,256]{1,0:T(8,128)(2,1)S(1)}, u32[]{:S(2)}, u32[]{:S(2)}) collective-permute-start(bf16[384,256]{1,0:T(8,128)(2,1)} %bitcast.7), channel_id=1, source_target_pairs={{0,8},{8,0},{1,9},{9,1},{2,10},{10,2},{3,11},{11,3},{4,12},{12,4},... | collective-permute-start | bytes 589832 | tf_op jit(solution)/shard_map/ppermute | solution.py:23
  25.4 4.7 %collective-permute-start.4 = (bf16[384,256]{1,0:T(8,128)(2,1)}, bf16[384,256]{1,0:T(8,128)(2,1)S(1)}, u32[]{:S(2)}, u32[]{:S(2)}) collective-permute-start(bf16[384,256]{1,0:T(8,128)(2,1)} %bitcast.8), channel_id=1, source_target_pairs={{0,64},{64,0},{32,96},{96,32},{128,192},{192,128},{160,224},{224,1... | collective-permute-start | bytes 589832 | tf_op jit(solution)/shard_map/ppermute | solution.py:23
  30.0 0.0 collective-permute-done.8.refs_10_
  30.0 0.0 copy-start
  30.0 2.3 %collective-permute-start.3 = (bf16[384,256]{1,0:T(8,128)(2,1)}, bf16[384,256]{1,0:T(8,128)(2,1)S(1)}, u32[]{:S(2)}, u32[]{:S(2)}) collective-permute-start(bf16[384,256]{1,0:T(8,128)(2,1)} %bitcast.9), channel_id=1, source_target_pairs={{0,4},{4,0},{1,5},{5,1},{2,6},{6,2},{3,7},{7,3},{8,12},{12,8},{9,1... | collective-permute-start | bytes 589832 | tf_op jit(solution)/shard_map/ppermute | solution.py:23
  32.4 0.0 collective-permute-done.7.refs_9_
  32.4 0.0 copy-start.1
  32.4 3.1 %collective-permute-start.2 = (bf16[384,256]{1,0:T(8,128)(2,1)}, bf16[384,256]{1,0:T(8,128)(2,1)S(1)}, u32[]{:S(2)}, u32[]{:S(2)}) collective-permute-start(bf16[384,256]{1,0:T(8,128)(2,1)} %bitcast.10), channel_id=1, source_target_pairs={{0,2},{2,0},{1,3},{3,1},{4,6},{6,4},{5,7},{7,5},{8,10},{10,8},{9,1... | collective-permute-start | bytes 589832 | tf_op jit(solution)/shard_map/ppermute | solution.py:23
  35.5 2.8 %collective-permute-done.6.refs_8_ = bf16[384,256]{1,0:T(8,128)(2,1)S(1)} collective-permute-done((bf16[384,256]{1,0:T(8,128)(2,1)}, bf16[384,256]{1,0:T(8,128)(2,1)S(1)}, u32[]{:S(2)}, u32[]{:S(2)}) %collective-permute-start.6) | collective-permute-done | bytes 196640 | tf_op jit(solution)/shard_map/ppermute | solution.py:23
  38.2 0.0 copy-start.2
  38.2 3.2 %collective-permute-start.1 = (bf16[384,256]{1,0:T(8,128)(2,1)}, bf16[384,256]{1,0:T(8,128)(2,1)S(1)}, u32[]{:S(2)}, u32[]{:S(2)}) collective-permute-start(bf16[384,256]{1,0:T(8,128)(2,1)} %bitcast.11), channel_id=1, source_target_pairs={{0,32},{32,0},{64,96},{96,64},{128,160},{160,128},{192,224},{224,1... | collective-permute-start | bytes 589832 | tf_op jit(solution)/shard_map/ppermute | solution.py:23
  41.4 0.0 collective-permute-done.5.refs_7_
  41.4 0.0 copy-start.3
  41.4 2.7 %collective-permute-start = (bf16[384,256]{1,0:T(8,128)(2,1)}, bf16[384,256]{1,0:T(8,128)(2,1)S(1)}, u32[]{:S(2)}, u32[]{:S(2)}) collective-permute-start(bf16[384,256]{1,0:T(8,128)(2,1)} %bitcast.12), channel_id=1, source_target_pairs={{0,1},{1,0},{2,3},{3,2},{4,5},{5,4},{6,7},{7,6},{8,9},{9,8},{10,11... | collective-permute-start | bytes 589832 | tf_op jit(solution)/shard_map/ppermute | solution.py:23
  44.2 0.0 collective-permute-done.4.refs_6_
  44.2 0.0 copy-start.4
  44.2 0.0 collective-permute-done.3.refs_5_
  44.2 0.0 copy-start.5
  44.2 0.0 collective-permute-done.2.refs_4_
  44.2 0.0 copy-start.6
  44.2 2.0 %collective-permute-done.1.refs_3_ = bf16[384,256]{1,0:T(8,128)(2,1)S(1)} collective-permute-done((bf16[384,256]{1,0:T(8,128)(2,1)}, bf16[384,256]{1,0:T(8,128)(2,1)S(1)}, u32[]{:S(2)}, u32[]{:S(2)}) %collective-permute-start.1) | collective-permute-done | bytes 196640 | tf_op jit(solution)/shard_map/ppermute | solution.py:23
  46.2 0.0 copy-start.7
  46.2 0.0 collective-permute-done.refs_2_
  46.2 0.0 copy-start.8
  46.2 0.0 copy-done
  46.2 0.0 copy-done.1
  46.2 0.0 copy-done.2
  46.2 0.0 copy-done.3
  46.2 0.0 copy-done.4
  46.3 0.0 copy-done.5
  46.3 0.0 copy-done.6
  46.3 0.6 %copy-done.7 = bf16[384,256]{1,0:T(8,128)(2,1)} copy-done((bf16[384,256]{1,0:T(8,128)(2,1)}, bf16[384,256]{1,0:T(8,128)(2,1)S(1)}, u32[]{:S(2)}) %copy-start.7) | copy-done | bytes 196632
  46.9 0.1 copy-done.8
  46.9 13.8 %shard_map.28 = bf16[384,768]{1,0:T(8,128)(2,1)} custom-call(bf16[384,768]{1,0:T(8,128)(2,1)} %bitcast.3, bf16[384,256]{1,0:T(8,128)(2,1)} %bitcast.13, bf16[384,256]{1,0:T(8,128)(2,1)} %copy-done.8, bf16[384,256]{1,0:T(8,128)(2,1)} %copy-done.7, bf16[384,256]{1,0:T(8,128)(2,1)} %copy-done.6, bf16[384,256]{1,0:T(8,128)(2,1)} %copy-done.5, ...), custom_call_target="tpu_custom_call" | custom-call | tf_op jit(solution)/shard_map/pallas_call | solution.py:66
Async XLA Ops:
  0.0 30.0 %collective-permute-start.8 = (bf16[384,256]{1,0:T(8,128)(2,1)}, bf16[384,256]{1,0:T(8,128)(2,1)S(1)}, u32[]{:S(2)}, u32[]{:S(2)}) collective-permute-start(bf16[384,256]{1,0:T(8,128)(2,1)} %bitcast.4), channel_id=1, source_target_pairs={{0,16},{16,0},{1,17},{17,1},{2,18},{18,2},{3,19},{19,3},{4,20},{20... | collective-permute-start | bytes 589832 | tf_op jit(solution)/shard_map/ppermute | solution.py:23
  8.3 24.1 %collective-permute-start.7 = (bf16[384,256]{1,0:T(8,128)(2,1)}, bf16[384,256]{1,0:T(8,128)(2,1)S(1)}, u32[]{:S(2)}, u32[]{:S(2)}) collective-permute-start(bf16[384,256]{1,0:T(8,128)(2,1)} %bitcast.5), channel_id=1, source_target_pairs={{0,256},{256,0},{32,288},{288,32},{64,320},{320,64},{96,352},{352,... | collective-permute-start | bytes 589832 | tf_op jit(solution)/shard_map/ppermute | solution.py:23
  18.9 19.3 %collective-permute-start.6 = (bf16[384,256]{1,0:T(8,128)(2,1)}, bf16[384,256]{1,0:T(8,128)(2,1)S(1)}, u32[]{:S(2)}, u32[]{:S(2)}) collective-permute-start(bf16[384,256]{1,0:T(8,128)(2,1)} %bitcast.6), channel_id=1, source_target_pairs={{0,128},{128,0},{32,160},{160,32},{64,192},{192,64},{96,224},{224,... | collective-permute-start | bytes 589832 | tf_op jit(solution)/shard_map/ppermute | solution.py:23
  22.9 18.5 %collective-permute-start.5 = (bf16[384,256]{1,0:T(8,128)(2,1)}, bf16[384,256]{1,0:T(8,128)(2,1)S(1)}, u32[]{:S(2)}, u32[]{:S(2)}) collective-permute-start(bf16[384,256]{1,0:T(8,128)(2,1)} %bitcast.7), channel_id=1, source_target_pairs={{0,8},{8,0},{1,9},{9,1},{2,10},{10,2},{3,11},{11,3},{4,12},{12,4},... | collective-permute-start | bytes 589832 | tf_op jit(solution)/shard_map/ppermute | solution.py:23
  25.4 18.8 %collective-permute-start.4 = (bf16[384,256]{1,0:T(8,128)(2,1)}, bf16[384,256]{1,0:T(8,128)(2,1)S(1)}, u32[]{:S(2)}, u32[]{:S(2)}) collective-permute-start(bf16[384,256]{1,0:T(8,128)(2,1)} %bitcast.8), channel_id=1, source_target_pairs={{0,64},{64,0},{32,96},{96,32},{128,192},{192,128},{160,224},{224,1... | collective-permute-start | bytes 589832 | tf_op jit(solution)/shard_map/ppermute | solution.py:23
  30.0 16.2 %copy-start = (bf16[384,256]{1,0:T(8,128)(2,1)}, bf16[384,256]{1,0:T(8,128)(2,1)S(1)}, u32[]{:S(2)}) copy-start(bf16[384,256]{1,0:T(8,128)(2,1)S(1)} %collective-permute-done.8.refs_10_) | copy-start | bytes 589828
  30.0 14.2 %collective-permute-start.3 = (bf16[384,256]{1,0:T(8,128)(2,1)}, bf16[384,256]{1,0:T(8,128)(2,1)S(1)}, u32[]{:S(2)}, u32[]{:S(2)}) collective-permute-start(bf16[384,256]{1,0:T(8,128)(2,1)} %bitcast.9), channel_id=1, source_target_pairs={{0,4},{4,0},{1,5},{5,1},{2,6},{6,2},{3,7},{7,3},{8,12},{12,8},{9,1... | collective-permute-start | bytes 589832 | tf_op jit(solution)/shard_map/ppermute | solution.py:23
  32.4 13.8 %copy-start.1 = (bf16[384,256]{1,0:T(8,128)(2,1)}, bf16[384,256]{1,0:T(8,128)(2,1)S(1)}, u32[]{:S(2)}) copy-start(bf16[384,256]{1,0:T(8,128)(2,1)S(1)} %collective-permute-done.7.refs_9_) | copy-start | bytes 589828
  32.4 11.8 %collective-permute-start.2 = (bf16[384,256]{1,0:T(8,128)(2,1)}, bf16[384,256]{1,0:T(8,128)(2,1)S(1)}, u32[]{:S(2)}, u32[]{:S(2)}) collective-permute-start(bf16[384,256]{1,0:T(8,128)(2,1)} %bitcast.10), channel_id=1, source_target_pairs={{0,2},{2,0},{1,3},{3,1},{4,6},{6,4},{5,7},{7,5},{8,10},{10,8},{9,1... | collective-permute-start | bytes 589832 | tf_op jit(solution)/shard_map/ppermute | solution.py:23
  38.2 8.0 %copy-start.2 = (bf16[384,256]{1,0:T(8,128)(2,1)}, bf16[384,256]{1,0:T(8,128)(2,1)S(1)}, u32[]{:S(2)}) copy-start(bf16[384,256]{1,0:T(8,128)(2,1)S(1)} %collective-permute-done.6.refs_8_) | copy-start | bytes 589828
  38.2 8.0 %collective-permute-start.1 = (bf16[384,256]{1,0:T(8,128)(2,1)}, bf16[384,256]{1,0:T(8,128)(2,1)S(1)}, u32[]{:S(2)}, u32[]{:S(2)}) collective-permute-start(bf16[384,256]{1,0:T(8,128)(2,1)} %bitcast.11), channel_id=1, source_target_pairs={{0,32},{32,0},{64,96},{96,64},{128,160},{160,128},{192,224},{224,1... | collective-permute-start | bytes 589832 | tf_op jit(solution)/shard_map/ppermute | solution.py:23
  41.4 4.8 %copy-start.3 = (bf16[384,256]{1,0:T(8,128)(2,1)}, bf16[384,256]{1,0:T(8,128)(2,1)S(1)}, u32[]{:S(2)}) copy-start(bf16[384,256]{1,0:T(8,128)(2,1)S(1)} %collective-permute-done.5.refs_7_) | copy-start | bytes 589828
  41.4 4.8 %collective-permute-start = (bf16[384,256]{1,0:T(8,128)(2,1)}, bf16[384,256]{1,0:T(8,128)(2,1)S(1)}, u32[]{:S(2)}, u32[]{:S(2)}) collective-permute-start(bf16[384,256]{1,0:T(8,128)(2,1)} %bitcast.12), channel_id=1, source_target_pairs={{0,1},{1,0},{2,3},{3,2},{4,5},{5,4},{6,7},{7,6},{8,9},{9,8},{10,11... | collective-permute-start | bytes 589832 | tf_op jit(solution)/shard_map/ppermute | solution.py:23
  44.2 2.1 %copy-start.4 = (bf16[384,256]{1,0:T(8,128)(2,1)}, bf16[384,256]{1,0:T(8,128)(2,1)S(1)}, u32[]{:S(2)}) copy-start(bf16[384,256]{1,0:T(8,128)(2,1)S(1)} %collective-permute-done.4.refs_6_) | copy-start | bytes 589828
  44.2 2.0 %copy-start.5 = (bf16[384,256]{1,0:T(8,128)(2,1)}, bf16[384,256]{1,0:T(8,128)(2,1)S(1)}, u32[]{:S(2)}) copy-start(bf16[384,256]{1,0:T(8,128)(2,1)S(1)} %collective-permute-done.3.refs_5_) | copy-start | bytes 589828
  44.2 2.0 %copy-start.6 = (bf16[384,256]{1,0:T(8,128)(2,1)}, bf16[384,256]{1,0:T(8,128)(2,1)S(1)}, u32[]{:S(2)}) copy-start(bf16[384,256]{1,0:T(8,128)(2,1)S(1)} %collective-permute-done.2.refs_4_) | copy-start | bytes 589828
  46.2 0.7 %copy-start.7 = (bf16[384,256]{1,0:T(8,128)(2,1)}, bf16[384,256]{1,0:T(8,128)(2,1)S(1)}, u32[]{:S(2)}) copy-start(bf16[384,256]{1,0:T(8,128)(2,1)S(1)} %collective-permute-done.1.refs_3_) | copy-start | bytes 589828
  46.2 0.7 %copy-start.8 = (bf16[384,256]{1,0:T(8,128)(2,1)}, bf16[384,256]{1,0:T(8,128)(2,1)S(1)}, u32[]{:S(2)}) copy-start(bf16[384,256]{1,0:T(8,128)(2,1)S(1)} %collective-permute-done.refs_2_) | copy-start | bytes 589828
